TPU v7x, 128 devices: a whole 4x4x4 slice. The times are simulated.
128 devices in a mesh: req: 8 (over z, core), mp: 16 (over x, y).
Axes of the slice: x: 4, y: 4, z: 4, core: 2. Of those that a mesh axis runs over, the one named last changes fastest.
Arguments:
- states: bfloat16 [8, 32, 16, 5120], P('req', None, 'mp'), may hold values from -6 to 6
- lengths: int32 [8, 4], replicated, may hold values from 1 to 509, as said below
- request_adapters: int32 [8, 4], replicated, may hold values from 0 to 7
- attention_norm_gain: float32 [5120], replicated, may hold values from 0.1 to 1.9
- query_weight: bfloat16 [5120, 4096], P(None, 'mp')
- key_weight: bfloat16 [5120, 1024], P(None, 'mp')
- value_weight: bfloat16 [5120, 1024], P(None, 'mp'), may hold values from -0.078125 to 0.078125
- output_weight: bfloat16 [4096, 5120], P('mp'), may hold values from -0.09375 to 0.09375
- adapter_down_attention: bfloat16 [5120, 384], replicated, may hold values from -0.078125 to 0.078125
- adapter_up_query: bfloat16 [128, 4096], P(None, 'mp'), may hold values from -0.5 to 0.5
- adapter_up_key_value: bfloat16 [2, 128, 1024], P(None, None, 'mp'), may hold values from -0.5 to 0.5
- adapter_down_output: bfloat16 [4096, 128], P('mp'), may hold values from -0.09375 to 0.09375
- adapter_up_output: bfloat16 [128, 5120], replicated, may hold values from -0.875 to 0.875
- feed_norm_gain: float32 [5120], replicated, may hold values from 0.1 to 1.9
- gate_up_weight: bfloat16 [2, 5120, 10240], P(None, 'req', 'mp'), may hold values from -0.078125 to 0.078125
- down_weight: bfloat16 [5120, 10240], P('req', 'mp'), may hold values from -0.0625 to 0.0625
- adapter_down_gate_up: bfloat16 [5120, 256], replicated, may hold values from -0.078125 to 0.078125
- adapter_up_gate_up: bfloat16 [2, 128, 10240], P(None, None, 'mp'), may hold values from -0.5 to 0.5
- adapter_down_feed: bfloat16 [10240, 128], P('mp'), may hold values from -0.0625 to 0.0625
- adapter_up_feed: bfloat16 [128, 5120], replicated, may hold values from -0.875 to 0.875
Outputs:
- layer_out: bfloat16 [8, 32, 16, 5120], P('req', None, 'mp')
Inputs may be any that keep to these rules, and one draw needn't show every extreme that they name: `lengths`: each request has at least one token; each row sums to at most 512, some row to exactly 512, and all rows together to exactly 2048; some request is 509 tokens long.
All inputs are finite; a program needn't handle non-finite values.
Results may differ from a plain program's by a relative error of at most 0.03.
Values may be sent and summed in bfloat16 or wider, within the bound.
No kernel may reach another device: no remote copies, remote signals or barrier semaphores. Data moves between devices by JAX's collectives and lax.ppermute only.
A program may use at most 128 MiB of HBM per device.

v0:
```python
import jax
import jax.numpy as jnp
from jax import lax
from jax.sharding import PartitionSpec as P

HEAD_SIZE = 128
ADAPTER_RANK = 16
WINDOW = 128
SINK = 4
EPSILON = 1e-05
ROPE_THETA = 1000000.0


def from_partner(shard, axis, stride):
    return lax.ppermute(shard, axis, [(i, i ^ 1 << stride) for i in range(lax.axis_size(axis))])


def slot_info(length_rows, adapter_rows, slot_ids):
    request_ends = jnp.cumsum(length_rows, axis=1, dtype=jnp.int32)
    starts = request_ends - length_rows
    count_req = length_rows.shape[1]
    request = jnp.sum(
        (slot_ids[:, None] >= request_ends).astype(jnp.int32), axis=1, dtype=jnp.int32
    )
    living = request < count_req
    matches = request[:, None] == jnp.arange(count_req, dtype=jnp.int32)[None, :]
    opening = jnp.sum(jnp.where(matches, starts, 0), axis=1, dtype=jnp.int32)
    position = jnp.where(living, slot_ids - opening, 0)
    segment = jnp.where(living, request, count_req + slot_ids)
    chosen = jnp.sum(jnp.where(matches, adapter_rows, 0), axis=1, dtype=jnp.int32)
    adapter_slot = jnp.where(living, chosen, -1)
    return (living, position, segment, adapter_slot)


def normalize(input_tokens, gain_vec):
    values = input_tokens.astype(jnp.float32)
    factor = lax.rsqrt(jnp.mean(values * values, axis=-1, keepdims=True) + EPSILON)
    return (values * factor * gain_vec).astype(jnp.bfloat16)


def adapter_select_mask(adapter_slot, adapter_column_count, adapter_rank_size):
    token_owner_request = jnp.arange(adapter_column_count, dtype=jnp.int32) // adapter_rank_size
    return (adapter_slot[:, None] == token_owner_request[None, :]).astype(jnp.float32)


def rotate(vectors, position):
    half_dim = vectors.shape[-1] // 2
    inverse = ROPE_THETA ** (-(jnp.arange(half_dim, dtype=jnp.float32) * (2.0 / vectors.shape[-1])))
    angles = position.astype(jnp.float32)[:, None] * inverse[None, :]
    cosine = jnp.cos(angles)[:, None, :]
    sine_part = jnp.sin(angles)[:, None, :]
    lower_half = vectors[..., :half_dim]
    upper_half = vectors[..., half_dim:]
    return jnp.concatenate(
        [
            lower_half * cosine - upper_half * sine_part,
            upper_half * cosine + lower_half * sine_part,
        ],
        axis=-1,
    )


def attend(queries, key_rows, value_rows, position, segment):
    key_heads = key_rows.shape[1]
    group_size = queries.shape[1] // key_heads
    token_count = queries.shape[0]
    grouped_queries = queries.reshape(token_count, key_heads, group_size, queries.shape[2])
    scores = jnp.einsum(
        "qkgd,skd->kgqs", grouped_queries, key_rows, preferred_element_type=jnp.float32
    ) * queries.shape[2] ** (-0.5)
    allowed = (segment[:, None] == segment[None, :]) & (position[None, :] <= position[:, None])
    allowed = allowed & (
        (position[:, None] - position[None, :] < WINDOW) | (position[None, :] < SINK)
    )
    scores = jnp.where(allowed[None, None], scores, -jnp.inf)
    highest = jnp.max(scores, axis=-1, keepdims=True)
    weights_raw = jnp.exp(scores - highest)
    weights = (weights_raw / jnp.sum(weights_raw, axis=-1, keepdims=True)).astype(jnp.bfloat16)
    blended = jnp.einsum("kgqs,skd->qkgd", weights, value_rows, preferred_element_type=jnp.float32)
    return blended.reshape(token_count, -1).astype(jnp.bfloat16)


def spread_rows(first_part, second_part):
    return (
        lax.all_gather(first_part, "mp", axis=0, tiled=True),
        lax.all_gather(second_part, "mp", axis=0, tiled=True),
    )


def sum_rows(term_fn, row_count):
    return lax.psum_scatter(
        term_fn(jnp.int32(0), lax.axis_size("mp") * row_count).astype(jnp.bfloat16),
        "mp",
        scatter_dimension=0,
        tiled=True,
    ).astype(jnp.float32)


def feed_forward(
    residual_stream,
    adapter_indicator,
    feed_norm_gain,
    adapter_down_gate_up,
    adapter_up_gate_up,
    gate_up_full,
    down_full,
    adapter_down_feed,
    adapter_up_feed,
):
    adapter_column_count = adapter_indicator.shape[1]
    model_width = residual_stream.shape[1]
    feed_input = normalize(residual_stream, feed_norm_gain)
    gate_terms = (
        jnp.dot(feed_input, adapter_down_gate_up, preferred_element_type=jnp.float32)
        * jnp.tile(adapter_indicator, (1, 2))
    ).astype(jnp.bfloat16)
    mlp_all, gate_adapter_ranks = spread_rows(feed_input, gate_terms)
    gate_activation = jnp.dot(
        mlp_all, gate_up_full[0], preferred_element_type=jnp.float32
    ) + jnp.dot(
        gate_adapter_ranks[:, :adapter_column_count],
        adapter_up_gate_up[0],
        preferred_element_type=jnp.float32,
    )
    up_projected = jnp.dot(mlp_all, gate_up_full[1], preferred_element_type=jnp.float32) + jnp.dot(
        gate_adapter_ranks[:, adapter_column_count:],
        adapter_up_gate_up[1],
        preferred_element_type=jnp.float32,
    )
    hidden_activation = (jax.nn.silu(gate_activation) * up_projected).astype(jnp.bfloat16)

    def down_term(first_row, row_count):
        projected_rows = lax.dot_general(
            hidden_activation,
            down_full,
            (((1,), (1,)), ((), ())),
            preferred_element_type=jnp.float32,
        )
        return jnp.concatenate(
            [
                projected_rows,
                jnp.dot(hidden_activation, adapter_down_feed, preferred_element_type=jnp.float32),
            ],
            axis=1,
        )

    summed = sum_rows(down_term, residual_stream.shape[0])
    down_adapter_ranks = (summed[:, model_width:] * adapter_indicator).astype(jnp.bfloat16)
    return (
        residual_stream.astype(jnp.float32)
        + summed[:, :model_width]
        + jnp.dot(down_adapter_ranks, adapter_up_feed, preferred_element_type=jnp.float32)
    )


def shards(
    states,
    lengths,
    request_adapters,
    attention_norm_gain,
    query_weight,
    key_weight,
    value_weight,
    output_weight,
    adapter_down_attention,
    adapter_up_query,
    adapter_up_key_value,
    adapter_down_output,
    adapter_up_output,
    feed_norm_gain,
    gate_up_weight,
    down_weight,
    adapter_down_gate_up,
    adapter_up_gate_up,
    adapter_down_feed,
    adapter_up_feed,
):
    mp_count = lax.axis_size("mp")
    group_index = lax.axis_index("req")
    mp_index = lax.axis_index("mp")
    slot_dev = states.shape[1]
    model_width = states.shape[3]
    adapter_column_count = adapter_up_output.shape[0]
    total_rows = slot_dev * mp_count
    gate_up_full, down_full = (
        lax.all_gather(gate_up_weight, "req", axis=1, tiled=True),
        lax.all_gather(down_weight, "req", axis=0, tiled=True),
    )
    local_rows = states.reshape(slot_dev, model_width)
    own_lengths = lax.dynamic_index_in_dim(lengths, group_index, 0, keepdims=False)
    own_adapters = lax.dynamic_index_in_dim(request_adapters, group_index, 0, keepdims=False)
    request_count = own_lengths.shape[0]
    local_slots = jnp.arange(slot_dev, dtype=jnp.int32) * mp_count + mp_index
    living, unused_pos, unused_seg, adapter_within = slot_info(
        jnp.broadcast_to(own_lengths[None, :], (slot_dev, request_count)),
        jnp.broadcast_to(own_adapters[None, :], (slot_dev, request_count)),
        local_slots,
    )
    indicator_within = adapter_select_mask(adapter_within, adapter_column_count, ADAPTER_RANK)
    normed_rows = normalize(local_rows, attention_norm_gain)
    down_adapter_terms = (
        jnp.dot(normed_rows, adapter_down_attention, preferred_element_type=jnp.float32)
        * jnp.tile(indicator_within, (1, 3))
    ).astype(jnp.bfloat16)
    normed_all, adapter_terms_all = spread_rows(normed_rows, down_adapter_terms)
    gathered = jnp.arange(total_rows, dtype=jnp.int32)
    gathered_slots = gathered % slot_dev * mp_count + gathered // slot_dev
    ignored, position_all, segment_all, unused = slot_info(
        jnp.broadcast_to(own_lengths[None, :], (total_rows, request_count)),
        jnp.broadcast_to(own_adapters[None, :], (total_rows, request_count)),
        gathered_slots,
    )
    query_projected = jnp.dot(
        normed_all, query_weight, preferred_element_type=jnp.float32
    ) + jnp.dot(
        adapter_terms_all[:, :adapter_column_count],
        adapter_up_query,
        preferred_element_type=jnp.float32,
    )
    key_projected = jnp.dot(normed_all, key_weight, preferred_element_type=jnp.float32) + jnp.dot(
        adapter_terms_all[:, adapter_column_count : 2 * adapter_column_count],
        adapter_up_key_value[0],
        preferred_element_type=jnp.float32,
    )
    value_projected = jnp.dot(
        normed_all, value_weight, preferred_element_type=jnp.float32
    ) + jnp.dot(
        adapter_terms_all[:, 2 * adapter_column_count :],
        adapter_up_key_value[1],
        preferred_element_type=jnp.float32,
    )
    kv_pair = jnp.stack([key_projected, value_projected])
    partner = from_partner(kv_pair.astype(jnp.bfloat16), "mp", 0).astype(kv_pair.dtype)
    parity = mp_index % 2
    joined = jnp.where(
        parity == 0,
        jnp.concatenate([kv_pair, partner], axis=2),
        jnp.concatenate([partner, kv_pair], axis=2),
    )
    key_projected = joined[0]
    value_projected = joined[1]
    queries = rotate(query_projected.reshape(total_rows, -1, HEAD_SIZE), position_all).astype(
        jnp.bfloat16
    )
    key_rows = rotate(key_projected.reshape(total_rows, -1, HEAD_SIZE), position_all).astype(
        jnp.bfloat16
    )
    value_rows = value_projected.reshape(total_rows, -1, HEAD_SIZE).astype(jnp.bfloat16)
    attention_output = attend(queries, key_rows, value_rows, position_all, segment_all)

    def out_term(first_row, row_count):
        return jnp.concatenate(
            [
                jnp.dot(attention_output, output_weight, preferred_element_type=jnp.float32),
                jnp.dot(attention_output, adapter_down_output, preferred_element_type=jnp.float32),
            ],
            axis=1,
        )

    summed = sum_rows(out_term, slot_dev)
    output_adapter_ranks = (summed[:, model_width:] * indicator_within).astype(jnp.bfloat16)
    residual_stream = (
        local_rows.astype(jnp.float32)
        + summed[:, :model_width]
        + jnp.dot(output_adapter_ranks, adapter_up_output, preferred_element_type=jnp.float32)
    ).astype(jnp.bfloat16)
    layer_result = feed_forward(
        residual_stream,
        indicator_within,
        feed_norm_gain,
        adapter_down_gate_up,
        adapter_up_gate_up,
        gate_up_full,
        down_full,
        adapter_down_feed,
        adapter_up_feed,
    )
    finished = jnp.where(living[:, None], layer_result, jnp.zeros_like(layer_result)).astype(
        jnp.bfloat16
    )
    return finished.reshape(1, slot_dev, 1, model_width)


def solution(mesh):
    placed = (
        P("req", None, "mp", None),
        P(),
        P(),
        P(),
        P(None, "mp"),
        P(None, "mp"),
        P(None, "mp"),
        P("mp", None),
        P(),
        P(None, "mp"),
        P(None, None, "mp"),
        P("mp", None),
        P(),
        P(),
        P(None, "req", "mp"),
        P("req", "mp"),
        P(),
        P(None, None, "mp"),
        P("mp", None),
        P(),
    )
    return jax.shard_map(
        shards, mesh=mesh, in_specs=placed, out_specs=P("req", None, "mp", None), check_vma=False
    )
```

profile of v0, /device:TPU:0, one launch (start us, length us, event | category | flops | bytes accessed | tf_op | source)
XLA Modules:
  0.0 374.3 jit_solution(9356517427873892993)
XLA Ops:
  7.4 1.3 fusion.17
  8.7 1.9 fusion.19
  10.5 0.0 all-gather.5.cloned.1.call-update
  10.6 0.0 reduce-scatter.3.cloned.1.call-start
  10.6 0.9 dynamic-slice_reduce_fusion
  11.5 0.1 broadcast_in_dim.40
  11.6 0.1 broadcast_in_dim.46
  11.8 0.1 select_reduce_fusion.1
  11.9 0.1 compare_convert_fusion
  12.0 0.3 copy-done.21
  12.3 2.9 fusion.12
  15.2 25.0 %all_gather.19 = bf16[512,384]{1,0:T(8,128)(2,1)S(1)} all-gather(bf16[32,384]{1,0:T(8,128)(2,1)S(1)} %fusion.12), channel_id=1, replica_groups=mesh['req'=8,'mp'=16] {'mp'}, dimensions={0}, use_global_device_ids=true | all-gather | bytes 417792 | tf_op jit(solution)/shard_map/all_gather | solution.py:86
  40.3 0.1 select_reduce_fusion
  40.4 1.2 fusion.16
  41.6 1.8 multiply_cosine_fusion
  43.4 26.8 %all-gather.5.cloned.1.call-done = bf16[512,5120]{1,0:T(8,128)(2,1)} async-done(((bf16[32,5120]{1,0:T(8,128)(2,1)}), bf16[512,5120]{1,0:T(8,128)(2,1)}) %all-gather.5.cloned.1.call-update) | async-done | bytes 5242896 | tf_op jit(solution)/shard_map/all_gather | solution.py:85
  70.2 4.5 %fusion.76 = f32[512,64]{0,1:T(8,128)S(1)} fusion(bf16[512,5120]{1,0:T(8,128)(2,1)} %all-gather.5.cloned.1.call-done, bf16[5120,64]{0,1:T(8,128)(2,1)} %param.26), kind=kOutput, calls=%fused_computation.140 | convolution fusion | flops 335544320 | bytes 6029312 | tf_op jit(solution)/shard_map/dot_general | solution.py:225
  74.7 0.2 fusion.10
  74.9 1.7 fusion.75
  76.6 0.2 fusion.11
  76.8 0.7 maximum_convert_fusion
  77.5 1.4 collective-permute-start
  78.9 1.6 fusion.77
  80.5 0.3 convolution_add_fusion.4
  80.8 0.8 fusion.73
  81.6 1.1 copy.44
  82.7 1.9 copy.45
  84.7 1.4 subtract_convert_fusion
  86.2 0.6 fusion.45
  86.8 0.6 fusion.74
  87.4 0.3 fusion.7
  87.7 0.5 convolution_convert_fusion.2
  88.3 1.6 convolution_convert_fusion
  89.8 0.3 convolution_convert_fusion.4
  90.1 2.7 pad_maximum_fusion
  92.8 0.0 reduce-scatter.3.cloned.1.call-update
  92.9 0.0 all-gather.9.cloned.1.call-start
  92.9 0.5 all-gather.9.cloned.1.call-update
  93.5 0.2 all-gather.7.cloned.1.call-start
  93.7 78.0 %reduce-scatter.3.cloned.1.call-done = bf16[32,5248]{1,0:T(8,128)(2,1)} async-done(((bf16[512,5248]{1,0:T(8,128)(2,1)}), bf16[32,5248]{1,0:T(8,128)(2,1)}) %reduce-scatter.3.cloned.1.call-update) | async-done | bytes 335888 | tf_op jit(solution)/shard_map/reduce_scatter | solution.py:91
  171.7 1.0 convert_element_type.118
  172.8 0.5 multiply_reduce_fusion
  173.3 0.9 multiply_convert_fusion
  174.1 0.0 all-gather.7.cloned.1.call-update
  174.2 0.0 all-gather.11.cloned.1.call-start
  174.2 0.5 all-gather.11.cloned.1.call-update
  174.7 0.0 reduce-scatter.5.cloned.1.call-start
  174.8 2.4 fusion.13
  177.2 23.4 %all_gather.22 = bf16[512,256]{1,0:T(8,128)(2,1)S(1)} all-gather(bf16[32,256]{1,0:T(8,128)(2,1)S(1)} %fusion.13), channel_id=1, replica_groups=mesh['req'=8,'mp'=16] {'mp'}, dimensions={0}, use_global_device_ids=true | all-gather | bytes 278528 | tf_op jit(solution)/shard_map/all_gather | solution.py:86
  200.6 0.0 all-gather.9.cloned.1.call-done
  200.7 29.8 %all-gather.7.cloned.1.call-done = bf16[512,5120]{1,0:T(8,128)(2,1)} async-done(((bf16[32,5120]{1,0:T(8,128)(2,1)}), bf16[512,5120]{1,0:T(8,128)(2,1)}) %all-gather.7.cloned.1.call-update) | async-done | bytes 5242896 | tf_op jit(solution)/shard_map/all_gather | solution.py:85
  230.5 8.7 %fusion.1 = f32[512,640]{1,0:T(8,128)S(1)} fusion(bf16[512,5120]{1,0:T(8,128)(2,1)} %all-gather.7.cloned.1.call-done, bf16[2,5120,640]{2,1,0:T(8,128)(2,1)} %all-gather.9.cloned.1.call-done), kind=kOutput, calls=%fused_computation.5 | convolution fusion | flops 3355443200 | bytes 13107200 | tf_op jit(solution)/shard_map/dot_general | solution.py:118
  239.2 1.2 convolution_add_fusion.3
  240.5 4.3 %fusion = f32[512,640]{1,0:T(8,128)S(1)} fusion(bf16[512,5120]{1,0:T(8,128)(2,1)S(1)} %copy-done.24, bf16[2,5120,640]{2,1,0:T(8,128)(2,1)S(1)} %copy-done.23), kind=kOutput, calls=%fused_computation.3 | convolution fusion | flops 3355443200 | bytes 13107200 | tf_op jit(solution)/shard_map/dot_general | solution.py:125
  244.8 0.5 fusion.9
  245.3 0.4 copy-done.7
  245.7 0.3 convolution_convert_fusion.3
  246.0 27.8 %all-gather.11.cloned.1.call-done = bf16[5120,640]{1,0:T(8,128)(2,1)} async-done(((bf16[640,640]{1,0:T(8,128)(2,1)}), bf16[5120,640]{1,0:T(8,128)(2,1)}) %all-gather.11.cloned.1.call-update) | async-done | bytes 6553616 | tf_op jit(solution)/shard_map/all_gather | solution.py:187
  273.9 7.3 %convolution_convert_fusion.1 = bf16[512,5120]{1,0:T(8,128)(2,1)S(1)} fusion(bf16[512,640]{1,0:T(8,128)(2,1)S(1)} %fusion.9, bf16[5120,640]{1,0:T(8,128)(2,1)} %all-gather.11.cloned.1.call-done), kind=kOutput, calls=%fused_computation.1 | convolution fusion | flops 3358064640 | bytes 12451840 | tf_op jit(solution)/shard_map/dot_general | solution.py:133
  281.2 2.7 pad_maximum_fusion.1
  283.9 0.6 copy-done.22
  284.6 79.0 %reduce-scatter.5.cloned.1.call-done = bf16[32,5248]{1,0:T(8,128)(2,1)} async-done(((bf16[512,5248]{1,0:T(8,128)(2,1)}), bf16[32,5248]{1,0:T(8,128)(2,1)}) %reduce-scatter.5.cloned.1.call-update) | async-done | bytes 335888 | tf_op jit(solution)/shard_map/reduce_scatter | solution.py:91
  363.5 1.0 convert_element_type.125
  364.5 2.4 fusion.6
  (71 shorter events, 0.4 us)
Async XLA Ops:
  7.4 80.9 %copy-start = (bf16[256,5120]{1,0:T(8,128)(2,1)S(1)}, bf16[256,5120]{1,0:T(8,128)(2,1)}, u32[]{:S(2)}) copy-start(bf16[256,5120]{1,0:T(8,128)(2,1)} %param.27) | copy-start | bytes 7864324
  7.4 62.8 %all-gather.5.cloned.1.call-start = ((), (), s32[]{:S(2)}) async-start(), calls=%async_computation.2 | async-start | bytes 5570560 | tf_op jit(solution)/shard_map/all_gather | solution.py:85
  10.6 161.2 %reduce-scatter.3.cloned.1.call-start = ((), (), s32[]{:S(2)}) async-start(), calls=%async_computation.3 | async-start | bytes 5709824 | tf_op jit(solution)/shard_map/reduce_scatter | solution.py:91
  11.8 31.6 %copy-start.15 = (s32[128]{0:T(128)}, s32[128]{0:T(128)S(1)}, u32[]{:S(2)}) copy-start(s32[128]{0:T(128)S(1)} %and_select_fusion) | copy-start | bytes 1540
  11.8 0.5 copy-start.21
  11.9 31.5 %copy-start.17 = (s32[32]{0:T(128)}, s32[32]{0:T(128)S(1)}, u32[]{:S(2)}) copy-start(s32[32]{0:T(128)S(1)} %broadcast_select_fusion) | copy-start | bytes 388
  40.3 3.1 copy-start.19
  40.4 3.0 copy-start.13
  43.4 31.3 %copy-start.11 = (bf16[2,128,64]{1,2,0:T(8,128)(2,1)S(1)}, bf16[2,128,64]{1,2,0:T(8,128)(2,1)}, u32[]{:S(2)}) copy-start(bf16[2,128,64]{1,2,0:T(8,128)(2,1)} %param.30) | copy-start | bytes 98308
  70.2 4.7 %copy-start.2 = (bf16[512,5120]{1,0:T(8,128)(2,1)S(1)}, bf16[512,5120]{1,0:T(8,128)(2,1)}, u32[]{:S(2)}) copy-start(bf16[512,5120]{1,0:T(8,128)(2,1)} %all-gather.5.cloned.1.call-done) | copy-start | bytes 15728644
  70.2 4.7 %copy-start.5 = (bf16[5120,64]{0,1:T(8,128)(2,1)S(1)}, bf16[5120,64]{0,1:T(8,128)(2,1)}, u32[]{:S(2)}) copy-start(bf16[5120,64]{0,1:T(8,128)(2,1)} %param.25) | copy-start | bytes 1966084
  74.9 4.0 %copy-start.25 = (bf16[5120,256]{1,0:T(8,128)(2,1)S(1)}, bf16[5120,256]{1,0:T(8,128)(2,1)}, u32[]{:S(2)}) copy-start(bf16[5120,256]{1,0:T(8,128)(2,1)} %param.24) | copy-start | bytes 7864324
  77.5 3.0 copy-start.9
  77.5 8.6 %collective-permute-start = (bf16[2,512,64]{1,2,0:T(8,128)(2,1)}, bf16[2,512,64]{1,2,0:T(8,128)(2,1)S(1)}, u32[]{:S(2)}, u32[]{:S(2)}) collective-permute-start(bf16[2,512,64]{1,2,0:T(8,128)(2,1)} %maximum_convert_fusion), channel_id=1, source_target_pairs={{0,1},{1,0},{2,3},{3,2},{4,5},{5,4},{6,7},{7,6},{8,9},{9,8},{10,11... | collective-permute-start | bytes 393224 | tf_op jit(solution)/shard_map/ppermute | solution.py:15
  84.7 1.5 copy-start.14
  84.7 1.5 copy-start.20
  84.7 2.1 copy-start.6
  88.3 1.6 copy-start.10
  92.8 79.9 %copy-start.3 = (bf16[1,32,1,5120]{3,1,2,0:T(8,128)(2,1)S(1)}, bf16[1,32,1,5120]{3,1,2,0:T(8,128)(2,1)}, u32[]{:S(2)}) copy-start(bf16[1,32,1,5120]{3,1,2,0:T(8,128)(2,1)} %param.20) | copy-start | bytes 983044
  92.8 79.9 %copy-start.4 = (bf16[128,5120]{1,0:T(8,128)(2,1)S(1)}, bf16[128,5120]{1,0:T(8,128)(2,1)}, u32[]{:S(2)}) copy-start(bf16[128,5120]{1,0:T(8,128)(2,1)} %param.32) | copy-start | bytes 3932164
  92.9 79.9 %copy-start.16 = (s32[128]{0:T(128)S(1)}, s32[128]{0:T(128)}, u32[]{:S(2)}) copy-start(s32[128]{0:T(128)} %copy-done.15) | copy-start | bytes 1540
  92.9 79.9 %copy-start.18 = (s32[32]{0:T(128)S(1)}, s32[32]{0:T(128)}, u32[]{:S(2)}) copy-start(s32[32]{0:T(128)} %copy-done.17) | copy-start | bytes 388
  92.9 80.4 %copy-start.12 = (f32[5120]{0:T(1024)S(1)}, f32[5120]{0:T(1024)}, u32[]{:S(2)}) copy-start(f32[5120]{0:T(1024)} %param.33) | copy-start | bytes 61444
  92.9 107.8 %all-gather.9.cloned.1.call-start = ((), (), s32[]{:S(2)}) async-start(), calls=%async_computation.5 | async-start | bytes 14745600 | tf_op jit(solution)/shard_map/all_gather | solution.py:186
  93.5 137.0 %all-gather.7.cloned.1.call-start = ((), (), s32[]{:S(2)}) async-start(), calls=%async_computation.4 | async-start | bytes 5570560 | tf_op jit(solution)/shard_map/all_gather | solution.py:85
  174.2 99.7 %all-gather.11.cloned.1.call-start = ((), (), s32[]{:S(2)}) async-start(), calls=%async_computation.6 | async-start | bytes 7372800 | tf_op jit(solution)/shard_map/all_gather | solution.py:187
  174.7 188.8 %reduce-scatter.5.cloned.1.call-start = ((), (), s32[]{:S(2)}) async-start(), calls=%async_computation.7 | async-start | bytes 5709824 | tf_op jit(solution)/shard_map/reduce_scatter | solution.py:91
  230.5 10.0 %copy-start.23 = (bf16[2,5120,640]{2,1,0:T(8,128)(2,1)S(1)}, bf16[2,5120,640]{2,1,0:T(8,128)(2,1)}, u32[]{:S(2)}) copy-start(bf16[2,5120,640]{2,1,0:T(8,128)(2,1)} %all-gather.9.cloned.1.call-done) | copy-start | bytes 39321604
  230.5 10.0 %copy-start.24 = (bf16[512,5120]{1,0:T(8,128)(2,1)S(1)}, bf16[512,5120]{1,0:T(8,128)(2,1)}, u32[]{:S(2)}) copy-start(bf16[512,5120]{1,0:T(8,128)(2,1)} %all-gather.7.cloned.1.call-done) | copy-start | bytes 15728644
  240.5 4.3 %copy-start.8 = (bf16[2,128,640]{2,1,0:T(8,128)(2,1)S(1)}, bf16[2,128,640]{2,1,0:T(8,128)(2,1)}, u32[]{:S(2)}) copy-start(bf16[2,128,640]{2,1,0:T(8,128)(2,1)} %param.37) | copy-start | bytes 983044
  244.8 0.9 copy-start.7
  283.9 0.6 copy-start.22
  284.5 82.4 %copy-start.1 = (bf16[256,5120]{1,0:T(8,128)(2,1)S(1)}, bf16[256,5120]{1,0:T(8,128)(2,1)}, u32[]{:S(2)}) copy-start(bf16[256,5120]{1,0:T(8,128)(2,1)} %param.27) | copy-start | bytes 7864324
Sparse Core Ops, SparseCore 0:
  10.7 59.4 all-gather.4
  93.0 78.7 reduce-scatter.2
  284.1 79.3 reduce-scatter.4
Sparse Core Ops, SparseCore 1:
  95.1 69.0 all-gather.8
  174.2 56.2 all-gather.6
  232.0 41.8 all-gather.10
where the time goes:
time: 375 us; the launch traced here: 374 us
  waiting for transfers between devices  243 us (65%)
  blocking collectives  48.4 us (13%)
  matrix products  41.9 us (11%)
  other arithmetic  17.8 us (5%)
  between operations  15.3 us (4%)
  local copies, waits for them, and re-layouts  6.46 us (2%)
    reduce_scatter x2, waiting for transfers between devices, sum_rows(): lax.psum_scatter(term_fn(jnp.int32(0), lax.axis_size('mp') * row_count).a...  157 us
    all_gather x2, waiting for transfers between devices, spread_rows(): lax.all_gather(first_part, 'mp', axis=0, tiled=True)  56.6 us
    all_gather x2, blocking collectives, spread_rows(): lax.all_gather(second_part, 'mp', axis=0, tiled=True)  48.4 us
    all_gather x1, waiting for transfers between devices, shards(): lax.all_gather(down_weight, 'req', axis=0, tiled=True)  27.8 us
    dot_general x1, matrix products, feed_forward(): jnp.dot(mlp_all, gate_up_full[0], preferred_element_type=jnp.float32)  8.72 us
  transfers between devices with their start and end apart: 7, of which 5 were waited for; matrix products, arithmetic and copies ran while one was open for 9% of the time, Pallas kernels for 0%

commit v1 on v0

--- a/solution.py
+++ b/solution.py
@@ -1,3 +1,4 @@
+import functools
 import jax
 import jax.numpy as jnp
 from jax import lax
@@ -9,6 +10,16 @@
 SINK = 4
 EPSILON = 1e-05
 ROPE_THETA = 1000000.0
+
+
+def _form_spans(local_block, row_dim):
+    big = jnp.stack(jax.lax.axis_size("req") * [local_block])
+    plain = jax.lax.all_to_all(big, "req", 0, 0)
+    view_out = jnp.concatenate(plain, axis=row_dim)
+    return view_out
+
+
+extend_chains = functools.partial(_form_spans, row_dim=0)
 
 
 def from_partner(shard, axis, stride):
@@ -184,7 +195,7 @@
     total_rows = slot_dev * mp_count
     gate_up_full, down_full = (
         lax.all_gather(gate_up_weight, "req", axis=1, tiled=True),
-        lax.all_gather(down_weight, "req", axis=0, tiled=True),
+        extend_chains(down_weight),
     )
     local_rows = states.reshape(slot_dev, model_width)
     own_lengths = lax.dynamic_index_in_dim(lengths, group_index, 0, keepdims=False)

time: 375 us -> 356 us (0.949)
  waiting for transfers between devices: 243 us -> 216 us
  starting transfers between devices: 1.82 us -> 6.68 us
    all_gather x1 -> x0, waiting for transfers between devices: 27.8 us -> none  [shards(): lax.all_gather(down_weight, 'req', axis=0, tiled=True)]
    all_to_all x0 -> x1, waiting for transfers between devices: none -> 12.9 us  [_form_spans(): plain = jax.lax.all_to_all(big, 'req', 0, 0)]
    all_gather x2, waiting for transfers between devices: 56.6 us -> 48.4 us  [spread_rows(): lax.all_gather(first_part, 'mp', axis=0, tiled=True)]
    all_to_all x0 -> x1, starting transfers between devices: none -> 4.9 us  [_form_spans(): plain = jax.lax.all_to_all(big, 'req', 0, 0)]
  transfers between devices with their start and end apart: 7 -> 7, of which waited for: 5 -> 5; matrix products, arithmetic and copies ran while one was open for 9% -> 10% of each run, Pallas kernels for 0% -> 0%
where the time goes in v1:
time: 356 us; the launch traced here: 355 us
  waiting for transfers between devices  216 us (61%)
  blocking collectives  48.2 us (14%)
  matrix products  41.9 us (12%)
  other arithmetic  17.9 us (5%)
  between operations  15.1 us (4%)
  local copies, waits for them, and re-layouts  9.47 us (3%)
  starting transfers between devices  6.68 us (2%)
    reduce_scatter x2, waiting for transfers between devices, sum_rows(): lax.psum_scatter(term_fn(jnp.int32(0), lax.axis_size('mp') * row_count).a...  154 us
    all_gather x2, waiting for transfers between devices, spread_rows(): lax.all_gather(first_part, 'mp', axis=0, tiled=True)  48.4 us
    all_gather x2, blocking collectives, spread_rows(): lax.all_gather(second_part, 'mp', axis=0, tiled=True)  48.2 us
    all_to_all x1, waiting for transfers between devices, _form_spans(): plain = jax.lax.all_to_all(big, 'req', 0, 0)  12.9 us
    dot_general x1, matrix products, feed_forward(): jnp.dot(mlp_all, gate_up_full[0], preferred_element_type=jnp.float32)  8.58 us
    dot_general x1, matrix products, down_term(): lax.dot_general(hidden_activation, down_full, (((1,), (1,)), ((), ())), p...  7.39 us
  transfers between devices with their start and end apart: 7, of which 5 were waited for; matrix products, arithmetic and copies ran while one was open for 10% of the time, Pallas kernels for 0%

profile of v1, /device:TPU:0, one launch (start us, length us, event | category | flops | bytes accessed | tf_op | source)
XLA Modules:
  0.0 355.2 jit_solution(3544653466798567951)
XLA Ops:
  7.4 1.3 fusion.17
  8.7 1.9 fusion.19
  10.5 0.0 all-gather.4.cloned.1.call-update
  10.6 0.0 reduce-scatter.3.cloned.1.call-start
  10.6 0.9 dynamic-slice_reduce_fusion
  11.5 0.1 broadcast_in_dim.40
  11.6 0.1 broadcast_in_dim.46
  11.8 0.1 select_reduce_fusion.1
  11.9 0.1 compare_convert_fusion
  12.0 0.4 copy-done.23
  12.4 2.9 fusion.12
  15.3 25.0 %all_gather.16 = bf16[512,384]{1,0:T(8,128)(2,1)S(1)} all-gather(bf16[32,384]{1,0:T(8,128)(2,1)S(1)} %fusion.12), channel_id=1, replica_groups=mesh['req'=8,'mp'=16] {'mp'}, dimensions={0}, use_global_device_ids=true | all-gather | bytes 417792 | tf_op jit(solution)/shard_map/all_gather | solution.py:97
  40.4 0.1 select_reduce_fusion
  40.5 1.2 fusion.16
  41.6 1.9 multiply_cosine_fusion
  43.5 26.7 %all-gather.4.cloned.1.call-done = bf16[512,5120]{1,0:T(8,128)(2,1)} async-done(((bf16[32,5120]{1,0:T(8,128)(2,1)}), bf16[512,5120]{1,0:T(8,128)(2,1)}) %all-gather.4.cloned.1.call-update) | async-done | bytes 5242896 | tf_op jit(solution)/shard_map/all_gather | solution.py:96
  70.2 4.5 %fusion.76 = f32[512,64]{0,1:T(8,128)S(1)} fusion(bf16[512,5120]{1,0:T(8,128)(2,1)} %all-gather.4.cloned.1.call-done, bf16[5120,64]{0,1:T(8,128)(2,1)} %param.26), kind=kOutput, calls=%fused_computation.140 | convolution fusion | flops 335544320 | bytes 6029312 | tf_op jit(solution)/shard_map/dot_general | solution.py:236
  74.7 0.2 fusion.10
  74.9 1.7 fusion.75
  76.6 0.2 fusion.11
  76.8 0.7 maximum_convert_fusion
  77.5 1.4 collective-permute-start
  78.9 1.6 fusion.77
  80.5 0.3 convolution_add_fusion.4
  80.8 0.8 fusion.73
  81.6 1.1 copy.44
  82.8 2.0 copy.45
  84.7 1.4 subtract_convert_fusion
  86.2 0.6 fusion.45
  86.8 0.6 fusion.74
  87.4 0.3 fusion.7
  87.7 0.5 convolution_convert_fusion.2
  88.3 1.6 convolution_convert_fusion
  89.9 0.3 convolution_convert_fusion.4
  90.1 2.7 pad_maximum_fusion
  92.9 0.0 reduce-scatter.3.cloned.1.call-update
  92.9 0.0 all-gather.8.cloned.1.call-start
  92.9 0.5 all-gather.8.cloned.1.call-update
  93.5 0.2 all-gather.6.cloned.1.call-start
  93.7 78.0 %reduce-scatter.3.cloned.1.call-done = bf16[32,5248]{1,0:T(8,128)(2,1)} async-done(((bf16[512,5248]{1,0:T(8,128)(2,1)}), bf16[32,5248]{1,0:T(8,128)(2,1)}) %reduce-scatter.3.cloned.1.call-update) | async-done | bytes 335888 | tf_op jit(solution)/shard_map/reduce_scatter | solution.py:102
  171.7 1.0 convert_element_type.118
  172.8 0.5 multiply_reduce_fusion
  173.3 0.9 multiply_convert_fusion
  174.1 0.0 all-gather.6.cloned.1.call-update
  174.2 3.3 stack.11
  177.4 4.9 %all-to-all-start = ((bf16[8,640,640]{2,1,0:T(8,128)(2,1)}), bf16[8,640,640]{2,1,0:T(8,128)(2,1)}, u32[]{:S(2)}, u32[]{:S(2)}) async-start(bf16[8,640,640]{2,1,0:T(8,128)(2,1)} %stack.11), calls=%async_computation.1 | async-start | bytes 13107200 | tf_op jit(solution)/shard_map/all_to_all | solution.py:17
  182.4 0.0 reduce-scatter.5.cloned.1.call-start
  182.4 2.4 fusion.13
  184.9 23.1 %all_gather.19 = bf16[512,256]{1,0:T(8,128)(2,1)S(1)} all-gather(bf16[32,256]{1,0:T(8,128)(2,1)S(1)} %fusion.13), channel_id=1, replica_groups=mesh['req'=8,'mp'=16] {'mp'}, dimensions={0}, use_global_device_ids=true | all-gather | bytes 278528 | tf_op jit(solution)/shard_map/all_gather | solution.py:97
  208.0 0.0 all-gather.8.cloned.1.call-done
  208.1 21.7 %all-gather.6.cloned.1.call-done = bf16[512,5120]{1,0:T(8,128)(2,1)} async-done(((bf16[32,5120]{1,0:T(8,128)(2,1)}), bf16[512,5120]{1,0:T(8,128)(2,1)}) %all-gather.6.cloned.1.call-update) | async-done | bytes 5242896 | tf_op jit(solution)/shard_map/all_gather | solution.py:96
  229.8 8.6 %fusion.1 = f32[512,640]{1,0:T(8,128)S(1)} fusion(bf16[512,5120]{1,0:T(8,128)(2,1)} %all-gather.6.cloned.1.call-done, bf16[2,5120,640]{2,1,0:T(8,128)(2,1)} %all-gather.8.cloned.1.call-done), kind=kOutput, calls=%fused_computation.5 | convolution fusion | flops 3355443200 | bytes 13107200 | tf_op jit(solution)/shard_map/dot_general | solution.py:129
  238.3 1.3 convolution_add_fusion.3
  239.6 4.3 %fusion = f32[512,640]{1,0:T(8,128)S(1)} fusion(bf16[512,5120]{1,0:T(8,128)(2,1)S(1)} %copy-done.26, bf16[2,5120,640]{2,1,0:T(8,128)(2,1)S(1)} %copy-done.25), kind=kOutput, calls=%fused_computation.3 | convolution fusion | flops 3355443200 | bytes 13107200 | tf_op jit(solution)/shard_map/dot_general | solution.py:136
  243.9 0.5 fusion.9
  244.4 12.9 %all-to-all-done = bf16[8,640,640]{2,1,0:T(8,128)(2,1)} async-done(((bf16[8,640,640]{2,1,0:T(8,128)(2,1)}), bf16[8,640,640]{2,1,0:T(8,128)(2,1)}, u32[]{:S(2)}, u32[]{:S(2)}) %all-to-all-start) | async-done | bytes 6553632 | tf_op jit(solution)/shard_map/all_to_all | solution.py:17
  257.3 7.4 %convolution_convert_fusion.1 = bf16[512,5120]{1,0:T(8,128)(2,1)S(1)} fusion(bf16[512,640]{1,0:T(8,128)(2,1)S(1)} %fusion.9, bf16[5120,640]{1,0:T(8,128)(2,1)} %bitcast.25), kind=kOutput, calls=%fused_computation.1 | convolution fusion | flops 3358064640 | bytes 12451840 | tf_op jit(solution)/shard_map/dot_general | solution.py:144
  264.7 0.3 convolution_convert_fusion.3
  265.1 2.7 pad_maximum_fusion.1
  267.8 0.0 reduce-scatter.5.cloned.1.call-update
  267.8 0.6 copy-done.24
  268.5 76.2 %reduce-scatter.5.cloned.1.call-done = bf16[32,5248]{1,0:T(8,128)(2,1)} async-done(((bf16[512,5248]{1,0:T(8,128)(2,1)}), bf16[32,5248]{1,0:T(8,128)(2,1)}) %reduce-scatter.5.cloned.1.call-update) | async-done | bytes 335888 | tf_op jit(solution)/shard_map/reduce_scatter | solution.py:102
  344.7 1.0 convert_element_type.125
  345.7 2.4 fusion.6
  (75 shorter events, 0.4 us)
Async XLA Ops:
  7.4 80.9 %copy-start = (bf16[256,5120]{1,0:T(8,128)(2,1)S(1)}, bf16[256,5120]{1,0:T(8,128)(2,1)}, u32[]{:S(2)}) copy-start(bf16[256,5120]{1,0:T(8,128)(2,1)} %param.27) | copy-start | bytes 7864324
  7.4 62.8 %all-gather.4.cloned.1.call-start = ((), (), s32[]{:S(2)}) async-start(), calls=%async_computation.3 | async-start | bytes 5570560 | tf_op jit(solution)/shard_map/all_gather | solution.py:96
  10.6 161.2 %reduce-scatter.3.cloned.1.call-start = ((), (), s32[]{:S(2)}) async-start(), calls=%async_computation.4 | async-start | bytes 5709824 | tf_op jit(solution)/shard_map/reduce_scatter | solution.py:102
  11.8 31.7 %copy-start.17 = (s32[128]{0:T(128)}, s32[128]{0:T(128)S(1)}, u32[]{:S(2)}) copy-start(s32[128]{0:T(128)S(1)} %and_select_fusion) | copy-start | bytes 1540
  11.8 0.6 copy-start.23
  11.9 31.6 %copy-start.19 = (s32[32]{0:T(128)}, s32[32]{0:T(128)S(1)}, u32[]{:S(2)}) copy-start(s32[32]{0:T(128)S(1)} %broadcast_select_fusion) | copy-start | bytes 388
  15.3 59.4 %copy-start.13 = (bf16[2,128,64]{1,2,0:T(8,128)(2,1)S(1)}, bf16[2,128,64]{1,2,0:T(8,128)(2,1)}, u32[]{:S(2)}) copy-start(bf16[2,128,64]{1,2,0:T(8,128)(2,1)} %param.30) | copy-start | bytes 98308
  40.3 3.2 copy-start.21
  40.5 3.0 copy-start.15
  70.2 4.7 %copy-start.2 = (bf16[512,5120]{1,0:T(8,128)(2,1)S(1)}, bf16[512,5120]{1,0:T(8,128)(2,1)}, u32[]{:S(2)}) copy-start(bf16[512,5120]{1,0:T(8,128)(2,1)} %all-gather.4.cloned.1.call-done) | copy-start | bytes 15728644
  70.2 4.7 %copy-start.7 = (bf16[5120,64]{0,1:T(8,128)(2,1)S(1)}, bf16[5120,64]{0,1:T(8,128)(2,1)}, u32[]{:S(2)}) copy-start(bf16[5120,64]{0,1:T(8,128)(2,1)} %param.25) | copy-start | bytes 1966084
  74.7 4.2 %copy-start.27 = (bf16[5120,256]{1,0:T(8,128)(2,1)S(1)}, bf16[5120,256]{1,0:T(8,128)(2,1)}, u32[]{:S(2)}) copy-start(bf16[5120,256]{1,0:T(8,128)(2,1)} %param.24) | copy-start | bytes 7864324
  77.5 3.0 copy-start.11
  77.5 8.6 %collective-permute-start = (bf16[2,512,64]{1,2,0:T(8,128)(2,1)}, bf16[2,512,64]{1,2,0:T(8,128)(2,1)S(1)}, u32[]{:S(2)}, u32[]{:S(2)}) collective-permute-start(bf16[2,512,64]{1,2,0:T(8,128)(2,1)} %maximum_convert_fusion), channel_id=1, source_target_pairs={{0,1},{1,0},{2,3},{3,2},{4,5},{5,4},{6,7},{7,6},{8,9},{9,8},{10,11... | collective-permute-start | bytes 393224 | tf_op jit(solution)/shard_map/ppermute | solution.py:26
  84.7 1.5 copy-start.16
  84.7 1.5 copy-start.22
  84.7 2.1 copy-start.8
  88.3 1.6 copy-start.12
  92.8 79.9 %copy-start.4 = (bf16[1,32,1,5120]{3,1,2,0:T(8,128)(2,1)S(1)}, bf16[1,32,1,5120]{3,1,2,0:T(8,128)(2,1)}, u32[]{:S(2)}) copy-start(bf16[1,32,1,5120]{3,1,2,0:T(8,128)(2,1)} %param.20) | copy-start | bytes 983044
  92.8 79.9 %copy-start.5 = (bf16[128,5120]{1,0:T(8,128)(2,1)S(1)}, bf16[128,5120]{1,0:T(8,128)(2,1)}, u32[]{:S(2)}) copy-start(bf16[128,5120]{1,0:T(8,128)(2,1)} %param.32) | copy-start | bytes 3932164
  92.8 79.9 %copy-start.18 = (s32[128]{0:T(128)S(1)}, s32[128]{0:T(128)}, u32[]{:S(2)}) copy-start(s32[128]{0:T(128)} %copy-done.17) | copy-start | bytes 1540
  92.8 79.9 %copy-start.20 = (s32[32]{0:T(128)S(1)}, s32[32]{0:T(128)}, u32[]{:S(2)}) copy-start(s32[32]{0:T(128)} %copy-done.19) | copy-start | bytes 388
  92.8 80.4 %copy-start.14 = (f32[5120]{0:T(1024)S(1)}, f32[5120]{0:T(1024)}, u32[]{:S(2)}) copy-start(f32[5120]{0:T(1024)} %param.33) | copy-start | bytes 61444
  92.9 81.3 %copy-start.6 = (bf16[640,640]{1,0:T(8,128)(2,1)S(1)}, bf16[640,640]{1,0:T(8,128)(2,1)}, u32[]{:S(2)}) copy-start(bf16[640,640]{1,0:T(8,128)(2,1)} %param.35) | copy-start | bytes 2457604
  92.9 115.2 %all-gather.8.cloned.1.call-start = ((), (), s32[]{:S(2)}) async-start(), calls=%async_computation.6 | async-start | bytes 14745600 | tf_op jit(solution)/shard_map/all_gather | solution.py:197
  93.5 136.3 %all-gather.6.cloned.1.call-start = ((), (), s32[]{:S(2)}) async-start(), calls=%async_computation.5 | async-start | bytes 5570560 | tf_op jit(solution)/shard_map/all_gather | solution.py:96
  177.4 5.0 %copy-start.3 = (bf16[32,5120]{1,0:T(8,128)(2,1)S(1)}, bf16[32,5120]{1,0:T(8,128)(2,1)}, u32[]{:S(2)}) copy-start(bf16[32,5120]{1,0:T(8,128)(2,1)} %multiply_convert_fusion) | copy-start | bytes 983044
  177.4 79.9 %all-to-all-start = ((bf16[8,640,640]{2,1,0:T(8,128)(2,1)}), bf16[8,640,640]{2,1,0:T(8,128)(2,1)}, u32[]{:S(2)}, u32[]{:S(2)}) async-start(bf16[8,640,640]{2,1,0:T(8,128)(2,1)} %stack.11), calls=%async_computation.1 | async-start | bytes 13107200 | tf_op jit(solution)/shard_map/all_to_all | solution.py:17
  182.4 162.3 %reduce-scatter.5.cloned.1.call-start = ((), (), s32[]{:S(2)}) async-start(), calls=%async_computation.7 | async-start | bytes 5709824 | tf_op jit(solution)/shard_map/reduce_scatter | solution.py:102
  229.7 9.9 %copy-start.25 = (bf16[2,5120,640]{2,1,0:T(8,128)(2,1)S(1)}, bf16[2,5120,640]{2,1,0:T(8,128)(2,1)}, u32[]{:S(2)}) copy-start(bf16[2,5120,640]{2,1,0:T(8,128)(2,1)} %all-gather.8.cloned.1.call-done) | copy-start | bytes 39321604
  229.7 9.9 %copy-start.26 = (bf16[512,5120]{1,0:T(8,128)(2,1)S(1)}, bf16[512,5120]{1,0:T(8,128)(2,1)}, u32[]{:S(2)}) copy-start(bf16[512,5120]{1,0:T(8,128)(2,1)} %all-gather.6.cloned.1.call-done) | copy-start | bytes 15728644
  239.6 4.3 %copy-start.10 = (bf16[2,128,640]{2,1,0:T(8,128)(2,1)S(1)}, bf16[2,128,640]{2,1,0:T(8,128)(2,1)}, u32[]{:S(2)}) copy-start(bf16[2,128,640]{2,1,0:T(8,128)(2,1)} %param.37) | copy-start | bytes 983044
  257.3 7.4 %copy-start.9 = (bf16[640,128]{1,0:T(8,128)(2,1)S(1)}, bf16[640,128]{1,0:T(8,128)(2,1)}, u32[]{:S(2)}) copy-start(bf16[640,128]{1,0:T(8,128)(2,1)} %param.38) | copy-start | bytes 491524
  267.8 0.7 copy-start.24
  267.8 80.3 %copy-start.1 = (bf16[256,5120]{1,0:T(8,128)(2,1)S(1)}, bf16[256,5120]{1,0:T(8,128)(2,1)}, u32[]{:S(2)}) copy-start(bf16[256,5120]{1,0:T(8,128)(2,1)} %param.27) | copy-start | bytes 7864324
Sparse Core Ops, SparseCore 0:
  10.7 59.4 all-gather.3
  93.0 78.6 reduce-scatter.2
  267.9 76.6 reduce-scatter.4
Sparse Core Ops, SparseCore 1:
  95.1 69.0 all-gather.7
  174.2 55.5 all-gather.5
